TPU v7x, 256 devices: a whole 4x4x8 slice. The times are simulated.
256 devices in a mesh: orb: 8 (over z_lo, core), box: 32 (over x, y, z_hi).
Axes of the slice: x: 4, y: 4, z: 8 (z_hi: 2, z_lo: 4; z = z_hi * 4 + z_lo), core: 2. Of those that a mesh axis runs over, the one named last changes fastest.
Arguments:
- orbitals: bfloat16 [768, 256, 1000], P('orb', 'box'), may hold values from -6 to 6
- exchange_values: bfloat16 [768, 256, 1000], P('orb', 'box'), may hold values from -6 to 6
- local_values: float32 [256, 1000], P('box'), may hold values from -6 to 6
- coupling: bfloat16 [768, 768], P('orb'), may hold values from -0.21875 to 0.21875
- to_values_mat: float32 [10, 10], replicated, may hold values from -2 to 2
- to_coeffs_mat: float32 [10, 10], replicated, may hold values from -2 to 2
- laplace_blocks: float32 [3, 10, 10], replicated, may hold values from -2 to 2
- box_counts: int32 [32], P('box'), may hold values from 2 to 8, as said below
- kept_mask: int32 [256], P('box'), may hold values from 0 to 1, as said below
- send_list: int32 [32, 32], P('box'), may hold values from -1 to 7, as said below
- neighbour_pos: int32 [6, 256], P(None, 'box'), may hold values from -1 to 39, as said below
Outputs:
- h_orbitals: bfloat16 [768, 256, 1000], P('orb', 'box')
Inputs may be any that keep to these rules, and one draw needn't show every extreme that they name: Device d of box holds live boxes in slots 0 to box_counts[d] - 1 of its 8; some device holds 8. `kept_mask`: 1 only on live boxes; at most 4 ones in one device's range, and exactly 4 in some device's range. `send_list`: row q, entries p * 1 to p + 1 - 1: live slots of device q's range passed to device p, -1 for an empty entry; nothing to its own device; at most 1 to one device, exactly 1 to the devices whose index differs by one. `neighbour_pos`: Boxes that are not live have -1 on every face.
All inputs are finite; a program needn't handle non-finite values.
Results may differ from a plain program's by a relative error of at most 0.0031.
Values may be sent and summed in bfloat16 or wider, within the bound.
No kernel may reach another device: no remote copies, remote signals or barrier semaphores. Data moves between devices by JAX's collectives and lax.ppermute only.
A program may use at most 256 MiB of HBM per device.

v0:
```python
import jax
import jax.numpy as jnp
from jax import lax
from jax.sharding import PartitionSpec as P

KEEP = 4


def digit_of(width, order_k, place):
    idx = lax.iota(jnp.int32, width)
    return idx // order_k ** (2 - place) % order_k


def expand(mat, width, place):
    order_k = mat.shape[0]
    digit = digit_of(width, order_k, place)
    ks = lax.iota(jnp.int32, order_k)
    left = (digit[:, None] == ks[None, :]).astype(jnp.float32)
    right = (ks[:, None] == digit[None, :]).astype(jnp.float32)
    hp = lax.Precision.HIGHEST
    return jnp.dot(jnp.dot(left, mat, precision=hp), right, precision=hp)


def same_digit(width, order_k, place):
    digit = digit_of(width, order_k, place)
    return (digit[:, None] == digit[None, :]).astype(jnp.float32)


def kron3(a, b, c):
    width = a.shape[0] * b.shape[0] * c.shape[0]
    return expand(a, width, 0) * expand(b, width, 1) * expand(c, width, 2)


def at_place(mat, width, place):
    order_k = mat.shape[0]
    out = expand(mat, width, place)
    for other in range(3):
        if other != place:
            out = out * same_digit(width, order_k, other)
    return out


def split_bf16(mat):
    hi = lax.reduce_precision(mat, exponent_bits=8, mantissa_bits=7)
    lo = (mat - hi).astype(jnp.bfloat16)
    return (hi.astype(jnp.bfloat16), lo)


def dot_f32(a, b):
    return jnp.dot(a, b, preferred_element_type=jnp.float32)


def apply_bf16(rows, parts):
    hi, lo = parts
    return dot_f32(rows, hi) + dot_f32(rows, lo)


def apply_f32(rows, parts):
    hi, lo = parts
    rows_hi_f = lax.reduce_precision(rows, exponent_bits=8, mantissa_bits=7)
    rows_lo = (rows - rows_hi_f).astype(jnp.bfloat16)
    rows_hi = rows_hi_f.astype(jnp.bfloat16)
    return dot_f32(rows_hi, hi) + dot_f32(rows_hi, lo) + dot_f32(rows_lo, hi)


def pick(onehot, block):
    return jnp.einsum("sb,nbc->nsc", onehot, block, preferred_element_type=jnp.float32).astype(
        jnp.bfloat16
    )


def shards(
    orbitals,
    exchange_values,
    local_values,
    coupling,
    to_values_mat,
    to_coeffs_mat,
    laplace_blocks,
    box_counts,
    kept_mask,
    send_list,
    neighbour_pos,
):
    orb_dev, box_dev, width = orbitals.shape
    order_k = to_values_mat.shape[0]
    n_box = send_list.shape[1]
    rows = orb_dev * box_dev
    slots = send_list[0]
    box_ids = lax.iota(jnp.int32, box_dev)
    send_hot = (slots[:, None] == box_ids[None, :]).astype(jnp.bfloat16)
    outgoing = pick(send_hot, orbitals)
    incoming = lax.all_to_all(outgoing, "box", split_axis=1, concat_axis=1, tiled=True)
    values_t = split_bf16(kron3(to_values_mat, to_values_mat, to_values_mat).T)
    flat = orbitals.reshape(rows, width)
    values = apply_bf16(flat, values_t).reshape(orb_dev, box_dev, width)
    kept = kept_mask > 0
    rank = jnp.cumsum(kept.astype(jnp.int32)) - 1
    keep_ids = lax.iota(jnp.int32, KEEP)
    sel = kept[None, :] & (rank[None, :] == keep_ids[:, None])
    products = jnp.where(
        kept[None, :, None], exchange_values.astype(jnp.float32) * values, 0.0
    ).astype(jnp.bfloat16)
    compact = pick(sel.astype(jnp.bfloat16), products)
    gathered = lax.all_gather(compact.reshape(orb_dev, KEEP * width), "orb", axis=0, tiled=True)
    mixed = dot_f32(coupling, gathered).reshape(orb_dev, KEEP, width)
    self_f = sel.astype(jnp.float32)
    exchange = mixed[:, 0:1, :] * self_f[0][None, :, None]
    for k in range(1, KEEP):
        exchange = exchange + mixed[:, k : k + 1, :] * self_f[k][None, :, None]
    weighted = local_values[None, :, :] * values - exchange
    coeffs_t = split_bf16(kron3(to_coeffs_mat, to_coeffs_mat, to_coeffs_mat).T)
    potential = apply_f32(weighted.reshape(rows, width), coeffs_t)
    lap0 = laplace_blocks[0]
    centre = sum((at_place(lap0, width, place) for place in range(3)))
    kinetic = apply_bf16(flat, split_bf16(centre.T))
    remote_ids = lax.iota(jnp.int32, n_box)
    for which in range(3):
        for side in range(2):
            face_pos = neighbour_pos[2 * which + side]
            local_hot = (face_pos[:, None] == box_ids[None, :]).astype(jnp.bfloat16)
            remote_hot = (face_pos[:, None] - box_dev == remote_ids[None, :]).astype(jnp.bfloat16)
            moved = pick(local_hot, orbitals) + pick(remote_hot, incoming)
            face_mat = at_place(laplace_blocks[1 + side], width, which)
            kinetic = kinetic + apply_bf16(moved.reshape(rows, width), split_bf16(face_mat.T))
    total = (potential - 0.5 * kinetic).reshape(orb_dev, box_dev, width)
    live = box_ids < box_counts[0]
    total = jnp.where(live[None, :, None], total, 0.0)
    return total.astype(jnp.bfloat16)


def solution(mesh):
    return jax.shard_map(
        shards,
        mesh=mesh,
        in_specs=(
            P("orb", "box", None),
            P("orb", "box", None),
            P("box", None),
            P("orb", None),
            P(),
            P(),
            P(),
            P("box"),
            P("box"),
            P("box", None),
            P(None, "box"),
        ),
        out_specs=P("orb", "box", None),
        check_vma=False,
    )
```

profile of v0, /device:TPU:66, one launch (start us, length us, event | category | flops | bytes accessed | tf_op | source)
XLA Modules:
  0.0 403.2 jit_solution(18097941252706797543)
XLA Ops:
  11.1 1.8 fusion.207
  13.0 1.8 fusion.202
  14.8 2.2 multiply_multiply_fusion.1
  17.0 2.0 fusion.50
  19.0 3.6 add_bitcast_fusion
  22.7 3.9 copy.33
  26.6 3.1 fusion.162
  29.7 2.2 reshape.228
  31.9 2.1 convert_bitcast_fusion
  34.0 6.2 %copy.39 = bf16[96,32,1000]{2,0,1:T(8,128)(2,1)} copy(bf16[96,32,1000]{2,1,0:T(8,128)(2,1)S(1)} %convert_bitcast_fusion) | data formatting | bytes 12288000 | tf_op jit(solution)/shard_map/convert_element_type | solution.py:67
  40.2 12.6 %all-to-all-start = ((bf16[96,32,1000]{2,0,1:T(8,128)(2,1)}), bf16[96,32,1000]{2,0,1:T(8,128)(2,1)}, u32[]{:S(2)}, u32[]{:S(2)}) async-start(bf16[96,32,1000]{2,0,1:T(8,128)(2,1)} %copy.39), calls=%async_computation | async-start | bytes 12582912 | tf_op jit(solution)/shard_map/all_to_all | solution.py:93
  54.6 2.0 broadcast_bitcast_fusion.4
  57.6 3.8 copy.32
  66.4 3.8 fusion.203
  70.2 3.8 fusion.196
  74.0 3.8 fusion.198
  77.8 3.7 fusion.204
  81.6 3.7 fusion.197
  85.3 4.0 fusion.199
  89.3 1.8 fusion.206
  91.1 1.8 fusion.201
  93.0 1.8 fusion.205
  94.8 1.8 fusion.200
  96.7 3.3 fusion.10
  99.9 4.1 %fusion.53 = f32[1000,768]{1,0:T(8,128)} fusion(f32[1000,1000]{1,0:T(8,128)S(1)} %fusion.10, bf16[96,8,1000]{2,1,0:T(8,128)(2,1)S(1)} %copy-done), kind=kOutput, calls=%fused_computation.91 | convolution fusion | flops 1538000000 | bytes 8608000 | tf_op jit(solution)/shard_map/dot_general | solution.py:50
  104.1 4.2 %multiply_multiply_fusion = f32[1000,1000]{1,0:T(8,128)} fusion(f32[1000,1000]{1,0:T(8,128)S(1)} %fusion.206, f32[1000,1000]{1,0:T(8,128)S(1)} %fusion.201, f32[1000,10]{0,1:T(8,128)S(1)} %fusion.169, s32[1000]{0:T(1024)S(1)} %add_select_fusion), kind=kOutput, calls=%fused_computation.51 | convolution fusion | flops 122010000 | bytes 12044000 | tf_op jit(solution)/shard_map/dot_general | solution.py:21
  108.3 3.6 fusion.46
  111.9 118.3 %all-gather.2.cloned.1.call-done = bf16[768,4000]{1,0:T(8,128)(2,1)} async-done(((bf16[96,4000]{1,0:T(8,128)(2,1)}), bf16[768,4000]{1,0:T(8,128)(2,1)}) %all-gather.2.cloned.1.call-update) | async-done | bytes 6144016 | tf_op jit(solution)/shard_map/all_gather | solution.py:105
  230.2 5.1 %convolution_bitcast_fusion = f32[96,4000]{1,0:T(8,128)} fusion(bf16[96,768]{1,0:T(8,128)(2,1)S(1)} %copy-done.11, bf16[768,4000]{1,0:T(8,128)(2,1)} %all-gather.2.cloned.1.call-done), kind=kOutput, calls=%fused_computation.37 | convolution fusion | flops 589824000 | bytes 7827456 | tf_op jit(solution)/shard_map/dot_general | solution.py:50
  235.3 2.8 reshape.229
  239.6 2.1 broadcast_bitcast_fusion.2
  241.6 3.6 copy.35
  245.3 2.0 broadcast_bitcast_fusion.1
  247.3 3.5 copy.36
  250.8 2.0 broadcast_bitcast_fusion
  252.8 3.5 copy.37
  256.4 2.1 broadcast_bitcast_fusion.3
  258.4 3.7 copy.34
  262.1 7.7 %add_subtract_fusion = f32[768,1000]{0,1:T(8,128)S(1)} fusion(f32[768,1000]{0,1:T(8,128)} %copy.37, f32[768,1000]{0,1:T(8,128)} %copy.36, f32[768,1000]{0,1:T(8,128)} %copy.35, f32[768,1000]{0,1:T(8,128)} %copy.34, f32[768,1000]{0,1:T(8,128)} %copy.32, f32[768,1000]{0,1:T(8,128)} %add_bitcast_fusion, f32[768]{0:T(1024)S(1)} %mul.221, f32[768]{0:T(1024)S(1)} %mul.213, ...), kind=kLoop, calls=%fused_computation.67 | loop fusion | flops 6912000 | bytes 21516288 | tf_op jit(solution)/shard_map/sub | solution.py:111
  269.9 3.5 fusion.165
  273.3 3.5 fusion.48
  276.8 6.3 %fusion.135 = bf16[96,1000,8]{1,2,0:T(8,128)(2,1)S(1)} fusion(bf16[96,32,1000]{2,0,1:T(8,128)(2,1)} %all-to-all-done, s32[8]{0:T(128)S(1)} %get-tuple-element.19), kind=kOutput, calls=%fused_computation.163 | convolution fusion | flops 49920256 | bytes 7680032 | tf_op jit(solution)/shard_map/sb,nbc->nsc/dot_general | solution.py:67
  285.3 3.9 fusion.34
  289.2 3.9 fusion.59
  293.1 6.3 %fusion.120 = bf16[96,1000,8]{1,2,0:T(8,128)(2,1)S(1)} fusion(bf16[96,32,1000]{2,0,1:T(8,128)(2,1)} %all-to-all-done, s32[8]{0:T(128)S(1)} %get-tuple-element.18), kind=kOutput, calls=%fused_computation.158 | convolution fusion | flops 49920256 | bytes 7680032 | tf_op jit(solution)/shard_map/sb,nbc->nsc/dot_general | solution.py:67
  301.6 3.8 fusion.44
  305.4 3.8 fusion.54
  309.2 6.7 %fusion.132 = bf16[96,1000,8]{1,2,0:T(8,128)(2,1)S(1)} fusion(bf16[96,32,1000]{2,0,1:T(8,128)(2,1)} %all-to-all-done, s32[8]{0:T(128)S(1)} %get-tuple-element.20), kind=kOutput, calls=%fused_computation.162 | convolution fusion | flops 49920256 | bytes 7680032 | tf_op jit(solution)/shard_map/sb,nbc->nsc/dot_general | solution.py:67
  316.6 1.5 copy-done.8
  318.1 3.9 fusion.36
  322.0 3.8 fusion.58
  325.8 6.3 %fusion.129 = bf16[96,1000,8]{1,2,0:T(8,128)(2,1)S(1)} fusion(bf16[96,32,1000]{2,0,1:T(8,128)(2,1)} %all-to-all-done, s32[8]{0:T(128)S(1)} %get-tuple-element.21), kind=kOutput, calls=%fused_computation.161 | convolution fusion | flops 49920256 | bytes 7680032 | tf_op jit(solution)/shard_map/sb,nbc->nsc/dot_general | solution.py:67
  332.7 1.5 copy-done.7
  334.3 4.0 fusion.38
  338.3 3.9 fusion.57
  342.1 6.3 %fusion.126 = bf16[96,1000,8]{1,2,0:T(8,128)(2,1)S(1)} fusion(bf16[96,32,1000]{2,0,1:T(8,128)(2,1)} %all-to-all-done, s32[8]{0:T(128)S(1)} %get-tuple-element.22), kind=kOutput, calls=%fused_computation.160 | convolution fusion | flops 49920256 | bytes 7680032 | tf_op jit(solution)/shard_map/sb,nbc->nsc/dot_general | solution.py:67
  350.6 3.9 fusion.40
  354.5 3.7 fusion.56
  358.2 6.5 %fusion.123 = bf16[96,1000,8]{1,2,0:T(8,128)(2,1)S(1)} fusion(bf16[96,32,1000]{2,0,1:T(8,128)(2,1)} %all-to-all-done, s32[8]{0:T(128)S(1)} %get-tuple-element.23), kind=kOutput, calls=%fused_computation.159 | convolution fusion | flops 49920256 | bytes 7680032 | tf_op jit(solution)/shard_map/sb,nbc->nsc/dot_general | solution.py:67
  366.9 3.9 fusion.42
  370.8 3.7 fusion.55
  374.5 18.2 %fusion.21 = bf16[768,1000]{0,1:T(8,128)(2,1)} fusion(f32[768,1000]{0,1:T(8,128)} %fusion.59, f32[768,1000]{0,1:T(8,128)} %fusion.34, f32[768,1000]{0,1:T(8,128)} %fusion.58, f32[768,1000]{0,1:T(8,128)} %fusion.36, f32[768,1000]{0,1:T(8,128)} %fusion.57, f32[768,1000]{0,1:T(8,128)} %fusion.38, f32[768,1000]{0,1:T(8,128)} %fusion.56, ...), kind=kOutput, calls=%fused_computation.66 | convolution fusion | flops 1554128000 | bytes 57760000 | tf_op jit(solution)/shard_map/dot_general | solution.py:50
  392.8 1.7 copy.48
  394.5 1.7 fusion.11
  (82 shorter events, 22.9 us)
Async XLA Ops:
  6.5 10.5 %copy-start = (bf16[96,8,1000]{2,1,0:T(8,128)(2,1)S(1)}, bf16[96,8,1000]{2,1,0:T(8,128)(2,1)}, u32[]{:S(2)}) copy-start(bf16[96,8,1000]{2,1,0:T(8,128)(2,1)} %param.11) | copy-start | bytes 4608004
  6.5 223.7 %all-gather.2.cloned.1.call-start = ((), (), s32[]{:S(2)}) async-start(), calls=%async_computation.1 | async-start | bytes 7077888 | tf_op jit(solution)/shard_map/all_gather | solution.py:105
  26.6 5.3 %copy-start.15 = (s32[1,32]{1,0:T(1,128)S(1)}, s32[1,32]{1,0:T(1,128)}, u32[]{:S(2)}) copy-start(s32[1,32]{1,0:T(1,128)} %param.20) | copy-start | bytes 388
  40.2 13.3 %copy-start.14 = (s32[6,8]{1,0:T(8,128)S(1)}, s32[6,8]{1,0:T(8,128)}, u32[]{:S(2)}) copy-start(s32[6,8]{1,0:T(8,128)} %param.21) | copy-start | bytes 580
  40.2 13.4 %copy-start.13 = (f32[3,10,10]{2,0,1:T(4,128)S(1)}, f32[3,10,10]{2,0,1:T(4,128)}, u32[]{:S(2)}) copy-start(f32[3,10,10]{2,0,1:T(4,128)} %param.17) | copy-start | bytes 3604
  40.2 14.4 %copy-start.12 = (f32[8,1000]{1,0:T(8,128)S(1)}, f32[8,1000]{1,0:T(8,128)}, u32[]{:S(2)}) copy-start(f32[8,1000]{1,0:T(8,128)} %param.13) | copy-start | bytes 96004
  40.2 236.7 %all-to-all-start = ((bf16[96,32,1000]{2,0,1:T(8,128)(2,1)}), bf16[96,32,1000]{2,0,1:T(8,128)(2,1)}, u32[]{:S(2)}, u32[]{:S(2)}) async-start(bf16[96,32,1000]{2,0,1:T(8,128)(2,1)} %copy.39), calls=%async_computation | async-start | bytes 12582912 | tf_op jit(solution)/shard_map/all_to_all | solution.py:93
  57.6 7.3 %copy-start.17 = (f32[10,10]{1,0:T(8,128)S(1)}, f32[10,10]{1,0:T(8,128)}, u32[]{:S(2)}) copy-start(f32[10,10]{1,0:T(8,128)} %param.16) | copy-start | bytes 1204
  108.3 121.9 %copy-start.11 = (bf16[96,768]{1,0:T(8,128)(2,1)S(1)}, bf16[96,768]{1,0:T(8,128)(2,1)}, u32[]{:S(2)}) copy-start(bf16[96,768]{1,0:T(8,128)(2,1)} %param.14) | copy-start | bytes 442372
  262.1 7.7 %copy-start.1 = (f32[1000,1000]{1,0:T(8,128)S(1)}, f32[1000,1000]{1,0:T(8,128)}, u32[]{:S(2)}) copy-start(f32[1000,1000]{1,0:T(8,128)} %multiply_multiply_fusion) | copy-start | bytes 12000004
  269.8 3.5 copy-start.3
  283.1 2.2 copy-start.10
  299.4 2.2 copy-start.9
  316.0 2.2 copy-start.8
  332.1 2.2 copy-start.7
  348.5 2.2 copy-start.6
  364.7 2.2 copy-start.5
  370.8 3.7 copy-start.2
  370.8 3.7 copy-start.4
  392.8 1.7 copy-start.16
Sparse Core Ops, SparseCore 0:
  32.0 198.1 all-gather.1
where the time goes:
time: 411 us; the launch traced here: 403 us
  matrix products  190 us (46%)
  waiting for transfers between devices  118 us (29%)
  local copies, waits for them, and re-layouts  56.3 us (14%)
  between operations  14.7 us (4%)
  starting transfers between devices  12.6 us (3%)
  other arithmetic  10.9 us (3%)
    all_gather x1, waiting for transfers between devices, shards(): lax.all_gather(compact.reshape(orb_dev, KEEP * width), 'orb', axis=0, til...  118 us
    dot_general x20, matrix products, dot_f32(): return jnp.dot(a, b, preferred_element_type=jnp.float32)  89.9 us
    dot_general x30, matrix products, expand(): return jnp.dot(jnp.dot(left, mat, precision=hp), right, precision=hp)  53.2 us
    dot_general x14, matrix products, pick(): jnp.einsum('sb,nbc->nsc', onehot, block, preferred_element_type=jnp.float32)  47.4 us
    mul x12, local copies, waits for them, and re-layouts, shards(): exchange = exchange + mixed[:, k:k + 1, :] * self_f[k][None, :, None]  17.1 us
    all_to_all x1, starting transfers between devices, shards(): lax.all_to_all(outgoing, 'box', split_axis=1, concat_axis=1, tiled=True)  12.6 us
    unnamed x40, local copies, waits for them, and re-layouts  9.54 us
  transfers between devices with their start and end apart: 2, of which 1 were waited for; matrix products, arithmetic and copies ran while one was open for 28% of the time, Pallas kernels for 0%

commit v1 on v0

--- a/solution.py
+++ b/solution.py
@@ -102,7 +102,12 @@
         kept[None, :, None], exchange_values.astype(jnp.float32) * values, 0.0
     ).astype(jnp.bfloat16)
     compact = pick(sel.astype(jnp.bfloat16), products)
-    gathered = lax.all_gather(compact.reshape(orb_dev, KEEP * width), "orb", axis=0, tiled=True)
+    gathered = jnp.concatenate(
+        lax.all_to_all(
+            jnp.stack([compact.reshape(orb_dev, KEEP * width)] * lax.axis_size("orb")), "orb", 0, 0
+        ),
+        axis=0,
+    )
     mixed = dot_f32(coupling, gathered).reshape(orb_dev, KEEP, width)
     self_f = sel.astype(jnp.float32)
     exchange = mixed[:, 0:1, :] * self_f[0][None, :, None]

time: 411 us -> 471 us (1.15)
  the two profiles are of different devices: /device:TPU:66 before, /device:TPU:130 now
where the time goes in v1:
time: 471 us; the launch traced here: 462 us
  matrix products  190 us (40%)
  waiting for transfers between devices  184 us (39%)
  local copies, waits for them, and re-layouts  58.8 us (12%)
  starting transfers between devices  17.4 us (4%)
  other arithmetic  10.9 us (2%)
    all_to_all x1, waiting for transfers between devices, shards(): lax.all_to_all(jnp.stack([compact.reshape(orb_dev, KEEP * width)] * lax.a...  127 us
    dot_general x20, matrix products, dot_f32(): return jnp.dot(a, b, preferred_element_type=jnp.float32)  89.8 us
    all_to_all x1, waiting for transfers between devices, shards(): lax.all_to_all(outgoing, 'box', split_axis=1, concat_axis=1, tiled=True)  57 us
    dot_general x30, matrix products, expand(): return jnp.dot(jnp.dot(left, mat, precision=hp), right, precision=hp)  53.1 us
    dot_general x14, matrix products, pick(): jnp.einsum('sb,nbc->nsc', onehot, block, preferred_element_type=jnp.float32)  47.3 us
    mul x12, local copies, waits for them, and re-layouts, shards(): exchange = exchange + mixed[:, k:k + 1, :] * self_f[k][None, :, None]  17 us
    all_to_all x1, starting transfers between devices, shards(): lax.all_to_all(outgoing, 'box', split_axis=1, concat_axis=1, tiled=True)  12.5 us
    unnamed x40, local copies, waits for them, and re-layouts  9.55 us
  transfers between devices with their start and end apart: 2, of which 2 were waited for; matrix products, arithmetic and copies ran while one was open for 24% of the time, Pallas kernels for 0%

profile of v1, /device:TPU:130, one launch (start us, length us, event | category | flops | bytes accessed | tf_op | source)
XLA Modules:
  0.0 462.4 jit_solution(17265827093058635703)
XLA Ops:
  4.6 1.8 fusion.207
  6.4 1.8 fusion.202
  8.3 2.2 multiply_multiply_fusion.1
  10.5 2.0 fusion.50
  12.5 3.6 add_bitcast_fusion
  16.1 3.9 copy.33
  20.1 3.0 fusion.162
  24.4 3.5 stack.3
  27.9 4.9 %all-to-all-start = ((bf16[8,96,4000]{2,1,0:T(8,128)(2,1)}), bf16[8,96,4000]{2,1,0:T(8,128)(2,1)}, u32[]{:S(2)}, u32[]{:S(2)}) async-start(bf16[8,96,4000]{2,1,0:T(8,128)(2,1)} %stack.3), calls=%async_computation | async-start | bytes 12582912 | tf_op jit(solution)/shard_map/all_to_all | solution.py:106
  33.5 2.1 convert_bitcast_fusion
  35.6 6.2 %copy.39 = bf16[96,32,1000]{2,0,1:T(8,128)(2,1)} copy(bf16[96,32,1000]{2,1,0:T(8,128)(2,1)S(1)} %convert_bitcast_fusion) | data formatting | bytes 12288000 | tf_op jit(solution)/shard_map/convert_element_type | solution.py:67
  42.9 2.1 broadcast_bitcast_fusion.4
  45.0 126.8 %all-to-all-done = bf16[8,96,4000]{2,1,0:T(8,128)(2,1)} async-done(((bf16[8,96,4000]{2,1,0:T(8,128)(2,1)}), bf16[8,96,4000]{2,1,0:T(8,128)(2,1)}, u32[]{:S(2)}, u32[]{:S(2)}) %all-to-all-start) | async-done | bytes 6144032 | tf_op jit(solution)/shard_map/all_to_all | solution.py:106
  171.8 12.5 %all-to-all-start.1 = ((bf16[96,32,1000]{2,0,1:T(8,128)(2,1)}), bf16[96,32,1000]{2,0,1:T(8,128)(2,1)}, u32[]{:S(2)}, u32[]{:S(2)}) async-start(bf16[96,32,1000]{2,0,1:T(8,128)(2,1)} %copy.39), calls=%async_computation.1 | async-start | bytes 12582912 | tf_op jit(solution)/shard_map/all_to_all | solution.py:93
  185.2 3.7 copy.32
  194.0 3.8 fusion.203
  197.8 3.8 fusion.196
  201.6 3.7 fusion.198
  205.3 3.8 fusion.204
  209.1 3.7 fusion.197
  212.8 4.0 fusion.199
  216.8 1.8 fusion.206
  218.6 1.8 fusion.201
  220.5 1.8 fusion.205
  222.3 1.8 fusion.200
  224.1 3.3 fusion.10
  227.4 4.1 fusion.53
  231.5 4.2 multiply_multiply_fusion
  235.8 3.6 fusion.46
  239.4 5.1 %convolution_bitcast_fusion = f32[96,4000]{1,0:T(8,128)} fusion(bf16[96,768]{1,0:T(8,128)(2,1)S(1)} %copy-done.11, bf16[768,4000]{1,0:T(8,128)(2,1)} %bitcast.9), kind=kOutput, calls=%fused_computation.37 | convolution fusion | flops 589824000 | bytes 7827456 | tf_op jit(solution)/shard_map/dot_general | solution.py:50
  244.5 2.8 reshape.231
  248.8 2.0 broadcast_bitcast_fusion.2
  250.8 3.6 copy.35
  254.4 2.0 broadcast_bitcast_fusion.1
  256.5 3.5 copy.36
  260.0 2.0 broadcast_bitcast_fusion
  262.0 3.5 copy.37
  265.5 2.0 broadcast_bitcast_fusion.3
  267.6 3.7 copy.34
  271.3 7.7 %add_subtract_fusion = f32[768,1000]{0,1:T(8,128)S(1)} fusion(f32[768,1000]{0,1:T(8,128)} %copy.37, f32[768,1000]{0,1:T(8,128)} %copy.36, f32[768,1000]{0,1:T(8,128)} %copy.35, f32[768,1000]{0,1:T(8,128)} %copy.34, f32[768,1000]{0,1:T(8,128)} %copy.32, f32[768,1000]{0,1:T(8,128)} %add_bitcast_fusion, f32[768]{0:T(1024)S(1)} %mul.221, f32[768]{0:T(1024)S(1)} %mul.213, ...), kind=kLoop, calls=%fused_computation.67 | loop fusion | flops 6912000 | bytes 21516288 | tf_op jit(solution)/shard_map/sub | solution.py:116
  279.0 3.5 fusion.165
  282.5 3.5 fusion.48
  286.0 57.0 %all-to-all-done.1 = bf16[96,32,1000]{2,0,1:T(8,128)(2,1)} async-done(((bf16[96,32,1000]{2,0,1:T(8,128)(2,1)}), bf16[96,32,1000]{2,0,1:T(8,128)(2,1)}, u32[]{:S(2)}, u32[]{:S(2)}) %all-to-all-start.1) | async-done | bytes 6144032 | tf_op jit(solution)/shard_map/all_to_all | solution.py:93
  343.0 6.3 %fusion.135 = bf16[96,1000,8]{1,2,0:T(8,128)(2,1)S(1)} fusion(bf16[96,32,1000]{2,0,1:T(8,128)(2,1)} %all-to-all-done.1, s32[8]{0:T(128)S(1)} %get-tuple-element.19), kind=kOutput, calls=%fused_computation.163 | convolution fusion | flops 49920256 | bytes 7680032 | tf_op jit(solution)/shard_map/sb,nbc->nsc/dot_general | solution.py:67
  351.5 3.9 fusion.34
  355.3 3.9 fusion.59
  359.3 6.3 %fusion.120 = bf16[96,1000,8]{1,2,0:T(8,128)(2,1)S(1)} fusion(bf16[96,32,1000]{2,0,1:T(8,128)(2,1)} %all-to-all-done.1, s32[8]{0:T(128)S(1)} %get-tuple-element.18), kind=kOutput, calls=%fused_computation.158 | convolution fusion | flops 49920256 | bytes 7680032 | tf_op jit(solution)/shard_map/sb,nbc->nsc/dot_general | solution.py:67
  367.7 3.8 fusion.44
  371.5 3.7 fusion.54
  375.3 6.7 %fusion.132 = bf16[96,1000,8]{1,2,0:T(8,128)(2,1)S(1)} fusion(bf16[96,32,1000]{2,0,1:T(8,128)(2,1)} %all-to-all-done.1, s32[8]{0:T(128)S(1)} %get-tuple-element.20), kind=kOutput, calls=%fused_computation.162 | convolution fusion | flops 49920256 | bytes 7680032 | tf_op jit(solution)/shard_map/sb,nbc->nsc/dot_general | solution.py:67
  384.1 3.9 fusion.36
  388.0 3.8 fusion.58
  391.8 6.3 %fusion.129 = bf16[96,1000,8]{1,2,0:T(8,128)(2,1)S(1)} fusion(bf16[96,32,1000]{2,0,1:T(8,128)(2,1)} %all-to-all-done.1, s32[8]{0:T(128)S(1)} %get-tuple-element.21), kind=kOutput, calls=%fused_computation.161 | convolution fusion | flops 49920256 | bytes 7680032 | tf_op jit(solution)/shard_map/sb,nbc->nsc/dot_general | solution.py:67
  400.2 4.0 fusion.38
  404.3 3.8 fusion.57
  408.0 6.3 %fusion.126 = bf16[96,1000,8]{1,2,0:T(8,128)(2,1)S(1)} fusion(bf16[96,32,1000]{2,0,1:T(8,128)(2,1)} %all-to-all-done.1, s32[8]{0:T(128)S(1)} %get-tuple-element.22), kind=kOutput, calls=%fused_computation.160 | convolution fusion | flops 49920256 | bytes 7680032 | tf_op jit(solution)/shard_map/sb,nbc->nsc/dot_general | solution.py:67
  416.5 3.8 fusion.40
  420.4 3.8 fusion.56
  424.2 6.5 %fusion.123 = bf16[96,1000,8]{1,2,0:T(8,128)(2,1)S(1)} fusion(bf16[96,32,1000]{2,0,1:T(8,128)(2,1)} %all-to-all-done.1, s32[8]{0:T(128)S(1)} %get-tuple-element.23), kind=kOutput, calls=%fused_computation.159 | convolution fusion | flops 49920256 | bytes 7680032 | tf_op jit(solution)/shard_map/sb,nbc->nsc/dot_general | solution.py:67
  432.9 3.9 fusion.42
  436.8 3.7 fusion.55
  440.5 18.3 %fusion.21 = bf16[768,1000]{0,1:T(8,128)(2,1)} fusion(f32[768,1000]{0,1:T(8,128)} %fusion.59, f32[768,1000]{0,1:T(8,128)} %fusion.34, f32[768,1000]{0,1:T(8,128)} %fusion.58, f32[768,1000]{0,1:T(8,128)} %fusion.36, f32[768,1000]{0,1:T(8,128)} %fusion.57, f32[768,1000]{0,1:T(8,128)} %fusion.38, f32[768,1000]{0,1:T(8,128)} %fusion.56, ...), kind=kOutput, calls=%fused_computation.66 | convolution fusion | flops 1554128000 | bytes 57760000 | tf_op jit(solution)/shard_map/dot_general | solution.py:50
  458.8 1.7 copy.48
  460.5 1.7 fusion.11
  (82 shorter events, 27.2 us)
Async XLA Ops:
  0.0 10.5 %copy-start = (bf16[96,8,1000]{2,1,0:T(8,128)(2,1)S(1)}, bf16[96,8,1000]{2,1,0:T(8,128)(2,1)}, u32[]{:S(2)}) copy-start(bf16[96,8,1000]{2,1,0:T(8,128)(2,1)} %param.11) | copy-start | bytes 4608004
  27.9 5.6 %copy-start.15 = (s32[1,32]{1,0:T(1,128)S(1)}, s32[1,32]{1,0:T(1,128)}, u32[]{:S(2)}) copy-start(s32[1,32]{1,0:T(1,128)} %param.20) | copy-start | bytes 388
  27.9 143.8 %all-to-all-start = ((bf16[8,96,4000]{2,1,0:T(8,128)(2,1)}), bf16[8,96,4000]{2,1,0:T(8,128)(2,1)}, u32[]{:S(2)}, u32[]{:S(2)}) async-start(bf16[8,96,4000]{2,1,0:T(8,128)(2,1)} %stack.3), calls=%async_computation | async-start | bytes 12582912 | tf_op jit(solution)/shard_map/all_to_all | solution.py:106
  35.6 6.2 %copy-start.14 = (s32[6,8]{1,0:T(8,128)S(1)}, s32[6,8]{1,0:T(8,128)}, u32[]{:S(2)}) copy-start(s32[6,8]{1,0:T(8,128)} %param.21) | copy-start | bytes 580
  35.6 6.2 %copy-start.13 = (f32[3,10,10]{2,0,1:T(4,128)S(1)}, f32[3,10,10]{2,0,1:T(4,128)}, u32[]{:S(2)}) copy-start(f32[3,10,10]{2,0,1:T(4,128)} %param.17) | copy-start | bytes 3604
  35.6 7.2 %copy-start.12 = (f32[8,1000]{1,0:T(8,128)S(1)}, f32[8,1000]{1,0:T(8,128)}, u32[]{:S(2)}) copy-start(f32[8,1000]{1,0:T(8,128)} %param.13) | copy-start | bytes 96004
  171.8 171.2 %all-to-all-start.1 = ((bf16[96,32,1000]{2,0,1:T(8,128)(2,1)}), bf16[96,32,1000]{2,0,1:T(8,128)(2,1)}, u32[]{:S(2)}, u32[]{:S(2)}) async-start(bf16[96,32,1000]{2,0,1:T(8,128)(2,1)} %copy.39), calls=%async_computation.1 | async-start | bytes 12582912 | tf_op jit(solution)/shard_map/all_to_all | solution.py:93
  185.2 7.3 %copy-start.17 = (f32[10,10]{1,0:T(8,128)S(1)}, f32[10,10]{1,0:T(8,128)}, u32[]{:S(2)}) copy-start(f32[10,10]{1,0:T(8,128)} %param.16) | copy-start | bytes 1204
  235.8 3.6 copy-start.11
  271.3 7.7 %copy-start.1 = (f32[1000,1000]{1,0:T(8,128)S(1)}, f32[1000,1000]{1,0:T(8,128)}, u32[]{:S(2)}) copy-start(f32[1000,1000]{1,0:T(8,128)} %multiply_multiply_fusion) | copy-start | bytes 12000004
  279.0 3.5 copy-start.3
  349.3 2.2 copy-start.10
  365.6 2.2 copy-start.9
  382.0 2.2 copy-start.8
  398.1 2.2 copy-start.7
  414.4 2.2 copy-start.6
  430.7 2.2 copy-start.5
  436.7 3.8 copy-start.2
  436.8 3.8 copy-start.4
  458.8 1.7 copy-start.16
